TPU v7x, 512 devices: a whole 4x8x8 slice. The times are simulated.
512 devices in a mesh: owner: 16 (over x, y_hi), beam: 32 (over y_lo, z, core).
Axes of the slice: x: 4, y: 8 (y_hi: 4, y_lo: 2; y = y_hi * 2 + y_lo), z: 8, core: 2. Of those that a mesh axis runs over, the one named last changes fastest.
Arguments:
- hidden: bfloat16 [4096, 8192], P('owner'), may hold values from -6 to 6
- norm_gain: bfloat16 [8192], replicated, may hold values from 0.099609375 to 1.8984375
- w_qkv: bfloat16 [8192, 10240], P('owner', 'beam'), may hold values from -0.0625 to 0.0625
- w_out: bfloat16 [8192, 8192], P('beam', 'owner'), may hold values from -0.125 to 0.125
- kv_cache: bfloat16 [16384, 2, 8, 1024], P(('owner', 'beam')), may hold values from -384 to 384
- lengths: int32 [4096], P('owner'), may hold values from 1 to 32, 98304 in all
- kept_parent_device: int32 [16384, 1], P('owner'), may hold values from 0 to 31; in each aligned block of 32 rows (0 to 31, 32 to 63, ...) at most 2 rows name the same one
- keep_block: int32 [16384], P('owner'), may hold values from 0 to 31
Outputs:
- mixed: bfloat16 [4096, 8192], P('owner', 'beam')
Inputs may be any that keep to these rules, and one draw needn't show every extreme that they name: `kept_parent_device`: in each aligned block of 32 entries (the new blocks of one device) no value appears more than 2 times, and some value appears exactly 2 times in some block. `lengths`: each entry is at least 1; the largest is exactly 32.
All inputs are finite; a program needn't handle non-finite values. No bound on the sum of `lengths` on one device may be relied on, other than what follows from the above.
Results may differ from a plain program's by a relative error of at most 0.024.
Values may be sent and summed in bfloat16 or wider, within the bound.
No kernel may reach another device: no remote copies, remote signals or barrier semaphores. Data moves between devices by JAX's collectives and lax.ppermute only.
A program may use at most 64 MiB of HBM per device.

v0:
```python
import jax
import jax.numpy as jnp
from jax import lax
from jax.sharding import Mesh
from jax.sharding import PartitionSpec as P

QH = 64
KVH = 8
HD = 128
CACHE = 32
PAGE = 8
QKV = 10240
OWNER = ("x", "yh")
BEAM = ("yl", "z", "c")
PAIR = ("yl", "z")


def rotary_embed(values, positions):
    half = values.shape[-1] // 2
    freqs = 500000.0 ** (-(jnp.arange(half, dtype=jnp.float32) * 2.0) / values.shape[-1])
    angles = positions.astype(jnp.float32)[:, None] * freqs[None, :]
    cosine = jnp.cos(angles)[:, None, :]
    sine = jnp.sin(angles)[:, None, :]
    first = values[..., :half]
    second = values[..., half:]
    return jnp.concatenate(
        [first * cosine - second * sine, second * cosine + first * sine], axis=-1
    )


def regroup(blocks):
    return lax.all_to_all(blocks, BEAM, split_axis=1, concat_axis=1, tiled=True)


def gather_rows(tile, axis, count):
    copies = jnp.broadcast_to(tile[None], (count,) + tile.shape)
    return lax.all_to_all(copies, axis, 0, 0, tiled=True).reshape((-1,) + tile.shape[1:])


def ring_near(piece, axis, count):
    ahead = [(i, (i + 1) % count) for i in range(count)]
    behind = [(i, (i - 1) % count) for i in range(count)]
    return (lax.ppermute(piece, axis, ahead), lax.ppermute(piece, axis, behind))


def ring_far(piece, near, axis, count):
    ahead = [(i, (i + 1) % count) for i in range(count)]
    behind = [(i, (i - 1) % count) for i in range(count)]
    from_left, from_right = near
    cut = piece.shape[0] // 2
    far = jnp.concatenate(
        [lax.ppermute(from_left[:cut], axis, ahead), lax.ppermute(from_right[cut:], axis, behind)],
        axis=0,
    )
    return [piece, from_right, far, from_left]


def attend(queries, fresh_key, value_new, keys, values, positions):
    beams = queries.shape[0]
    grouped_heads = queries.reshape(beams, KVH, QH // KVH, HD)
    scale_factor = HD ** (-0.5)
    scores = (
        jnp.einsum("bkgd,btkd->bkgt", grouped_heads, keys, preferred_element_type=jnp.float32)
        * scale_factor
    )
    local_beam_score = (
        jnp.einsum("rhap,rhp->rha", grouped_heads, fresh_key, preferred_element_type=jnp.float32)
        * scale_factor
    )
    valid = (jnp.arange(keys.shape[1], dtype=jnp.int32)[None, :] < positions[:, None])[
        :, None, None, :
    ]
    scores = jnp.where(valid, scores, -1e30)
    highest = jnp.maximum(jnp.max(scores, axis=-1), local_beam_score)
    weights = jnp.where(valid, jnp.exp(scores - highest[..., None]), 0.0)
    own_weight = jnp.exp(local_beam_score - highest)
    totals = jnp.sum(weights, axis=-1) + own_weight
    probs = (weights / totals[..., None]).astype(jnp.bfloat16)
    own_prob = (own_weight / totals).astype(jnp.bfloat16)
    output = jnp.einsum("bkgt,btkd->bkgd", probs, values, preferred_element_type=jnp.float32)
    output = (
        output
        + own_prob.astype(jnp.float32)[..., None] * value_new.astype(jnp.float32)[:, :, None, :]
    )
    return output.reshape(beams, QH * HD).astype(jnp.bfloat16)


def shards(hidden, norm_gain, w_qkv, w_out, kv_cache, lengths, kept_parent_device, keep_block):
    columns = lax.axis_size(BEAM)
    my_column = lax.axis_index(BEAM)
    grouped_row_block = hidden.shape[0]
    own_beams = grouped_row_block // columns
    cores = lax.axis_size("c")
    core = lax.axis_index("c")
    assert cores == 2
    halves = w_out.reshape(w_out.shape[0], cores, w_out.shape[1] // cores)
    mine = jnp.take(halves, core, axis=1)
    other = lax.ppermute(jnp.take(halves, 1 - core, axis=1), "c", [(0, 1), (1, 0)])
    w_local = jnp.where(
        core == 0, jnp.concatenate([mine, other], 0), jnp.concatenate([other, mine], 0)
    )
    floats = hidden.astype(jnp.float32)
    scale_rms = lax.rsqrt(jnp.mean(floats * floats, axis=-1, keepdims=True) + 1e-05)
    normed = (floats * scale_rms * norm_gain.astype(jnp.float32)).astype(jnp.bfloat16)
    xs = lax.axis_size("x")
    ys = lax.axis_size("yh")
    assert xs == 4 and ys == 4
    me = lax.axis_index("x")
    mine_y = lax.axis_index("yh")
    rows = w_qkv.shape[0]
    wide = 192
    stack = gather_rows(w_qkv[:, :wide], "yh", ys)
    by_x = ring_near(w_qkv[:, wide:], "x", xs)
    near = ring_near(stack, "x", xs)
    w_local, near, by_x = lax.optimization_barrier((w_local, near, by_x))
    w_pair = lax.all_gather(w_local[:, None], OWNER, axis=1, tiled=True)
    stack_b = jnp.concatenate(ring_far(w_qkv[:, wide:], by_x, "x", xs), axis=0)
    pieces_b = ring_far(stack_b, ring_near(stack_b, "yh", ys), "yh", ys)
    pieces_a = ring_far(stack, near, "x", xs)
    part_a = None
    for step, piece in enumerate(pieces_a):
        start = (me + step) % xs * ys * rows
        block = lax.dynamic_slice_in_dim(normed, start, ys * rows, axis=1)
        term = jnp.einsum(
            "jbd,dc->bjc",
            block.reshape(columns, own_beams, ys * rows),
            piece,
            preferred_element_type=jnp.float32,
        )
        part_a = term if part_a is None else part_a + term
    part_b = None
    for step, piece in enumerate(pieces_b):
        block = jnp.concatenate(
            [
                lax.dynamic_slice_in_dim(
                    normed, ((me + dx) % xs * ys + (mine_y + step) % ys) * rows, rows, axis=1
                )
                for dx in range(xs)
            ],
            axis=1,
        )
        term = jnp.einsum(
            "jbd,dc->bjc",
            block.reshape(columns, own_beams, xs * rows),
            piece,
            preferred_element_type=jnp.float32,
        )
        part_b = term if part_b is None else part_b + term
    projected = jnp.concatenate([part_a, part_b], axis=-1)
    own_qkv = regroup(projected.astype(jnp.bfloat16)).reshape(own_beams, QKV)
    blk_dev = kv_cache.shape[0]
    most_slots = max(2, 2 * blk_dev // columns)
    sources = kept_parent_device.reshape(columns, blk_dev)
    picked = keep_block.reshape(columns, blk_dev)
    is_mine = (sources == my_column).astype(jnp.int32)
    ranks = jnp.cumsum(is_mine, axis=1) - 1
    slot_ids = jnp.arange(most_slots, dtype=jnp.int32)
    chosen = is_mine[:, :, None] * (ranks[:, :, None] == slot_ids[None, None, :]).astype(jnp.int32)
    send_table = jnp.sum(chosen * picked[:, :, None], axis=1)
    outgoing = kv_cache[send_table.reshape(-1)].reshape((columns, most_slots) + kv_cache.shape[1:])
    incoming_blocks = lax.all_to_all(outgoing, BEAM, split_axis=0, concat_axis=0, tiled=True)
    own_sources = lax.dynamic_index_in_dim(sources, my_column, 0, keepdims=False)
    one_hot = (own_sources[:, None] == jnp.arange(columns, dtype=jnp.int32)[None, :]).astype(
        jnp.int32
    )
    earlier = jnp.cumsum(one_hot, axis=0) - one_hot
    arrival = jnp.sum(earlier * one_hot, axis=1)
    flat_blocks = incoming_blocks.reshape((columns * most_slots,) + kv_cache.shape[1:])
    moved = flat_blocks[own_sources * most_slots + arrival]
    moved = moved.reshape(own_beams, CACHE // PAGE, 2, PAGE, KVH, HD)
    keys = moved[:, :, 0].reshape(own_beams, CACHE, KVH, HD)
    values = moved[:, :, 1].reshape(own_beams, CACHE, KVH, HD)
    positions = lax.dynamic_slice_in_dim(lengths, my_column * own_beams, own_beams)
    query_cols = own_qkv[:, : QH * HD].reshape(own_beams, QH, HD).astype(jnp.float32)
    key_cols = own_qkv[:, QH * HD : (QH + KVH) * HD].reshape(own_beams, KVH, HD).astype(jnp.float32)
    value_new = own_qkv[:, (QH + KVH) * HD :].reshape(own_beams, KVH, HD)
    queries = rotary_embed(query_cols, positions).astype(jnp.bfloat16)
    fresh_key = rotary_embed(key_cols, positions).astype(jnp.bfloat16)
    attn = attend(queries, fresh_key, value_new, keys, values, positions)
    pairs = columns // cores
    pair_feats = attn.reshape(own_beams, pairs, 1, cores * attn.shape[1] // columns)
    doubled = jnp.broadcast_to(pair_feats, (own_beams, pairs, cores, pair_feats.shape[3]))
    head_rows = lax.all_to_all(
        doubled.reshape(own_beams, columns, pair_feats.shape[3]), BEAM, 1, 1, tiled=True
    )
    block = attn.shape[1] // columns
    partial = None
    for half in range(cores):
        term = (
            jnp.einsum(
                "bjh,hpc->jbpc",
                head_rows[:, :, half * block : (half + 1) * block],
                w_pair[half * block : (half + 1) * block],
                preferred_element_type=jnp.float32,
            )
            .astype(jnp.bfloat16)
            .astype(jnp.float32)
        )
        partial = term if partial is None else partial + term
    partial = partial.astype(jnp.bfloat16).reshape(grouped_row_block, pairs, block)
    spread = lax.all_to_all(partial.transpose(1, 0, 2), PAIR, 0, 0, tiled=True)
    return jnp.sum(spread.astype(jnp.float32), axis=0).astype(jnp.bfloat16)


def solution(mesh):
    sizes = dict(mesh.shape)
    parts = mesh.devices.reshape(4, sizes["owner"] // 4, 2, sizes["beam"] // 4, 2)
    view = Mesh(parts, OWNER + BEAM)
    return jax.shard_map(
        shards,
        mesh=view,
        in_specs=(
            P(OWNER, None),
            P(),
            P(OWNER, BEAM),
            P(BEAM, OWNER),
            P(OWNER + BEAM, None, None, None),
            P(OWNER),
            P(OWNER, None),
            P(OWNER),
        ),
        out_specs=P(OWNER, BEAM),
        check_vma=False,
    )
```

profile of v0, /device:TPU:56, one launch (start us, length us, event | category | flops | bytes accessed | tf_op | source)
XLA Modules:
  0.0 342.8 jit_solution(9053897651199613312)
XLA Ops:
  6.5 1.0 slice.65
  7.7 3.4 collective-permute-start.3
  11.1 3.7 %collective-permute-start.4 = (bf16[512,128]{1,0:T(8,128)(2,1)S(1)}, bf16[512,128]{1,0:T(8,128)(2,1)}, u32[]{:S(2)}, u32[]{:S(2)}) collective-permute-start(bf16[512,128]{1,0:T(8,128)(2,1)S(1)} %copy.153), channel_id=1, source_target_pairs={{0,384},{128,0},{256,128},{384,256},{1,385},{129,1},{257,129},{385... | collective-permute-start | bytes 393224 | tf_op jit(solution)/shard_map/ppermute | solution.py:43
  14.8 1.1 copy.103
  15.9 1.9 collective-permute-start
  18.8 7.0 %all-to-all-start = ((bf16[4,512,192]{1,2,0:T(8,128)(2,1)}), bf16[4,512,192]{1,2,0:T(8,128)(2,1)S(1)}, u32[]{:S(2)}, u32[]{:S(2)}) async-start(bf16[4,512,192]{1,2,0:T(8,128)(2,1)} %broadcast_in_dim.29), calls=%async_computation | async-start | bytes 1572864 | tf_op jit(solution)/shard_map/all_to_all | solution.py:37
  25.8 3.1 fusion
  30.4 5.3 %fusion.2 = bf16[256,8192]{1,0:T(8,128)(2,1)} fusion(bf16[256,8192]{1,0:T(8,128)(2,1)} %param.10, f32[8192]{0:T(1024)S(1)} %convert_element_type.98, f32[256]{0:T(256)S(1)} %add_rsqrt_fusion), kind=kLoop, calls=%fused_computation.6 | loop fusion | flops 8388608 | bytes 8422400 | tf_op jit(solution)/shard_map/convert_element_type | solution.py:104
  35.8 10.3 %all-to-all-done = bf16[4,512,192]{1,2,0:T(8,128)(2,1)S(1)} async-done(((bf16[4,512,192]{1,2,0:T(8,128)(2,1)}), bf16[4,512,192]{1,2,0:T(8,128)(2,1)S(1)}, u32[]{:S(2)}, u32[]{:S(2)}) %all-to-all-start) | async-done | bytes 786464 | tf_op jit(solution)/shard_map/all_to_all | solution.py:37
  46.2 1.9 collective-permute-start.1
  48.1 5.1 %collective-permute-start.2 = (bf16[2048,192]{0,1:T(8,128)(2,1)S(1)}, bf16[2048,192]{0,1:T(8,128)(2,1)}, u32[]{:S(2)}, u32[]{:S(2)}) collective-permute-start(bf16[2048,192]{0,1:T(8,128)(2,1)S(1)} %bitcast.157), channel_id=1, source_target_pairs={{0,384},{128,0},{256,128},{384,256},{1,385},{129,1},{257,129},{385... | collective-permute-start | bytes 2359304 | tf_op jit(solution)/shard_map/ppermute | solution.py:43
  53.2 4.4 %constant_dynamic-slice_fusion.16 = (bf16[256,512]{1,0:T(8,128)(2,1)}, bf16[256,512]{1,0:T(8,128)(2,1)}, bf16[256,512]{1,0:T(8,128)(2,1)}, bf16[256,512]{1,0:T(8...) fusion(bf16[256,8192]{1,0:T(8,128)(2,1)} %fusion.2, ...), kind=kLoop, calls=%fused_computation.145 | loop fusion | bytes 8388672 | tf_op jit(solution)/shard_map/dynamic_slice | solution.py:135
  57.7 1.8 dynamic-slice_bitcast_fusion.2
  63.1 1.1 slice.67
  64.2 3.1 collective-permute-start.5
  67.3 1.8 slice.68
  69.1 4.0 %collective-permute-start.6 = (bf16[1024,192]{0,1:T(8,128)(2,1)}, bf16[1024,192]{0,1:T(8,128)(2,1)}, u32[]{:S(2)}, u32[]{:S(2)}) collective-permute-start(bf16[1024,192]{0,1:T(8,128)(2,1)} %slice.68), channel_id=1, source_target_pairs={{0,384},{128,0},{256,128},{384,256},{1,385},{129,1},{257,129},{385... | collective-permute-start | bytes 1179656 | tf_op jit(solution)/shard_map/ppermute | solution.py:52
  73.1 2.3 fusion.42
  75.5 2.8 fusion.46
  78.3 1.5 slice.69
  79.8 1.9 collective-permute-start.7
  81.7 1.6 constant_dynamic-update-slice_fusion.3
  83.3 1.5 slice.70
  84.7 5.1 %collective-permute-start.8 = (bf16[256,128]{1,0:T(8,128)(2,1)}, bf16[256,128]{1,0:T(8,128)(2,1)}, u32[]{:S(2)}, u32[]{:S(2)}) collective-permute-start(bf16[256,128]{1,0:T(8,128)(2,1)} %slice.70), channel_id=1, source_target_pairs={{0,384},{128,0},{256,128},{384,256},{1,385},{129,1},{257,129},{385... | collective-permute-start | bytes 196616 | tf_op jit(solution)/shard_map/ppermute | solution.py:52
  89.9 1.5 constant_dynamic-update-slice_fusion.2
  92.1 1.5 constant_dynamic-update-slice_fusion.1
  93.5 1.6 constant_dynamic-update-slice_fusion
  95.1 4.2 %collective-permute-start.9 = (bf16[2048,128]{1,0:T(8,128)(2,1)}, bf16[2048,128]{1,0:T(8,128)(2,1)S(1)}, u32[]{:S(2)}, u32[]{:S(2)}) collective-permute-start(bf16[2048,128]{1,0:T(8,128)(2,1)} %constant_dynamic-update-slice_fusion), channel_id=1, source_target_pairs={{0,96},{32,0},{64,32},{96,64},{1,97},{33,1},{65,33},{97,65},{2,98}... | collective-permute-start | bytes 1572872 | tf_op jit(solution)/shard_map/ppermute | solution.py:43
  99.3 4.5 %collective-permute-start.10 = (bf16[2048,128]{1,0:T(8,128)(2,1)}, bf16[2048,128]{1,0:T(8,128)(2,1)S(1)}, u32[]{:S(2)}, u32[]{:S(2)}) collective-permute-start(bf16[2048,128]{1,0:T(8,128)(2,1)} %constant_dynamic-update-slice_fusion), channel_id=1, source_target_pairs={{0,32},{32,64},{64,96},{96,0},{1,33},{33,65},{65,97},{97,1},{2,34}... | collective-permute-start | bytes 1572872 | tf_op jit(solution)/shard_map/ppermute | solution.py:43
  103.8 2.0 fusion.44
  105.9 2.1 fusion.8
  108.0 14.6 %collective-permute-done.10 = bf16[2048,128]{1,0:T(8,128)(2,1)S(1)} collective-permute-done((bf16[2048,128]{1,0:T(8,128)(2,1)}, bf16[2048,128]{1,0:T(8,128)(2,1)S(1)}, u32[]{:S(2)}, u32[]{:S(2)}) %collective-permute-start.10) | collective-permute-done | bytes 524320 | tf_op jit(solution)/shard_map/ppermute | solution.py:43
  122.6 1.9 collective-permute-start.11
  124.6 4.8 %collective-permute-start.12 = (bf16[1024,128]{1,0:T(8,128)(2,1)S(1)}, bf16[1024,128]{1,0:T(8,128)(2,1)S(1)}, u32[]{:S(2)}, u32[]{:S(2)}) collective-permute-start(bf16[1024,128]{1,0:T(8,128)(2,1)S(1)} %slice.102), channel_id=1, source_target_pairs={{0,96},{32,0},{64,32},{96,64},{1,97},{33,1},{65,33},{97,65},{2,98}... | collective-permute-start | bytes 786440 | tf_op jit(solution)/shard_map/ppermute | solution.py:52
  131.1 8.0 %collective-permute-done.11 = bf16[1024,128]{1,0:T(8,128)(2,1)S(1)} collective-permute-done((bf16[1024,128]{1,0:T(8,128)(2,1)S(1)}, bf16[1024,128]{1,0:T(8,128)(2,1)S(1)}, u32[]{:S(2)}, u32[]{:S(2)}) %collective-permute-start.11) | collective-permute-done | bytes 262176 | tf_op jit(solution)/shard_map/ppermute | solution.py:52
  140.3 1.5 fusion.13
  142.6 40.6 %all-to-all-start.1 = ((bf16[8,32,320]{2,0,1:T(8,128)(2,1)}), bf16[8,32,320]{2,0,1:T(8,128)(2,1)S(1)}, u32[]{:S(2)}, u32[]{:S(2)}) async-start(bf16[8,32,320]{2,0,1:T(8,128)(2,1)} %pad_maximum_fusion), calls=%async_computation.1 | async-start | bytes 393216 | tf_op jit(solution)/shard_map/all_to_all | solution.py:32
  183.3 2.0 gather_fusion
  185.4 12.0 %all-to-all-done.1 = bf16[8,32,320]{2,0,1:T(8,128)(2,1)S(1)} async-done(((bf16[8,32,320]{2,0,1:T(8,128)(2,1)}), bf16[8,32,320]{2,0,1:T(8,128)(2,1)S(1)}, u32[]{:S(2)}, u32[]{:S(2)}) %all-to-all-start.1) | async-done | bytes 163872 | tf_op jit(solution)/shard_map/all_to_all | solution.py:32
  197.4 3.9 %all-to-all-start.2 = ((bf16[32,2,2,8,1024]{4,3,2,1,0:T(8,128)(2,1)}), bf16[32,2,2,8,1024]{4,3,2,1,0:T(8,128)(2,1)S(1)}, u32[]{:S(2)}, u32[]{:S(2)}) async-start(bf16[32,2,2,8,1024]{4,3,2,1,0:T(8,128)(2,1)} %bitcast.30), calls=%async_computation.2 | async-start | bytes 4194304 | tf_op jit(solution)/shard_map/all_to_all | solution.py:161
  202.9 48.5 %all-to-all-done.2 = bf16[32,2,2,8,1024]{4,3,2,1,0:T(8,128)(2,1)S(1)} async-done(((bf16[32,2,2,8,1024]{4,3,2,1,0:T(8,128)(2,1)}), bf16[32,2,2,8,1024]{4,3,2,1,0:T(8,128)(2,1)S(1)}, u32[]{:S(2)}, u32[]{:S(2)}) %all-to-all-start.2) | async-done | bytes 2097184 | tf_op jit(solution)/shard_map/all_to_all | solution.py:161
  251.4 1.6 gather_fusion.1
  253.0 1.5 copy.159
  256.0 19.9 %all_to_all.25 = bf16[8,32,512]{2,0,1:T(8,128)(2,1)S(1)} all-to-all(bf16[8,32,512]{2,0,1:T(8,128)(2,1)S(1)} %bitcast.155), channel_id=1, replica_groups=mesh['x'=4,'yh'=4,'yl'=2,'z'=8,'c'=2] {'yl','z','c'}, dimensions={1} | all-to-all | bytes 524288 | tf_op jit(solution)/shard_map/all_to_all | solution.py:183
  275.9 2.5 fusion.91
  279.9 1.2 copy.134
  281.8 53.2 %all_to_all.26 = bf16[16,256,256]{2,1,0:T(8,128)(2,1)S(1)} all-to-all(bf16[16,256,256]{2,1,0:T(8,128)(2,1)S(1)} %copy.135), channel_id=1, replica_groups=mesh['x'=4,'yh'=4,'yl'=2,'z'=8,'c'=2] {'yl','z'}, dimensions={0} | all-to-all | bytes 4194304 | tf_op jit(solution)/shard_map/all_to_all | solution.py:201
  335.0 1.0 reduce_sum.55
  (129 shorter events, 15.9 us)
Async XLA Ops:
  6.5 176.8 %copy-start = (bf16[32,2,8,1024]{3,2,1,0:T(8,128)(2,1)S(1)}, bf16[32,2,8,1024]{3,2,1,0:T(8,128)(2,1)}, u32[]{:S(2)}) copy-start(bf16[32,2,8,1024]{3,2,1,0:T(8,128)(2,1)} %param.14) | copy-start | bytes 3145732
  6.5 11.3 %slice-start = ((bf16[512,320]{0,1:T(8,128)(2,1)}), bf16[512,192]{0,1:T(8,128)(2,1)S(1)}, s32[]{:S(2)}) async-start(bf16[512,320]{0,1:T(8,128)(2,1)} %param.12), calls=%async_computation.6 | async-start | bytes 393216 | tf_op jit(solution)/shard_map/slice | solution.py:112
  7.7 55.4 %collective-permute-start.3 = (bf16[512,128]{1,0:T(8,128)(2,1)S(1)}, bf16[512,128]{1,0:T(8,128)(2,1)}, u32[]{:S(2)}, u32[]{:S(2)}) collective-permute-start(bf16[512,128]{1,0:T(8,128)(2,1)S(1)} %copy.153), channel_id=1, source_target_pairs={{0,128},{128,256},{256,384},{384,0},{1,129},{129,257},{257,385},{3... | collective-permute-start | bytes 393224 | tf_op jit(solution)/shard_map/ppermute | solution.py:43
  11.1 52.0 %collective-permute-start.4 = (bf16[512,128]{1,0:T(8,128)(2,1)S(1)}, bf16[512,128]{1,0:T(8,128)(2,1)}, u32[]{:S(2)}, u32[]{:S(2)}) collective-permute-start(bf16[512,128]{1,0:T(8,128)(2,1)S(1)} %copy.153), channel_id=1, source_target_pairs={{0,384},{128,0},{256,128},{384,256},{1,385},{129,1},{257,129},{385... | collective-permute-start | bytes 393224 | tf_op jit(solution)/shard_map/ppermute | solution.py:43
  14.8 11.0 %copy-start.21 = (bf16[8192]{0:T(1024)(128)(2,1)S(1)}, bf16[8192]{0:T(1024)(128)(2,1)}, u32[]{:S(2)}) copy-start(bf16[8192]{0:T(1024)(128)(2,1)} %param.11) | copy-start | bytes 49156
  15.9 45.2 %collective-permute-start = (bf16[256,256]{0,1:T(8,128)(2,1)S(1)}, bf16[256,256]{0,1:T(8,128)(2,1)S(1)}, u32[]{:S(2)}, u32[]{:S(2)}) collective-permute-start(bf16[256,256]{0,1:T(8,128)(2,1)S(1)} %get-tuple-element.59), channel_id=1, source_target_pairs={{0,1},{1,0},{2,3},{3,2},{4,5},{5,4},{6,7},{7,6},{8,9},{9,8},{10,11... | collective-permute-start | bytes 393224 | tf_op jit(solution)/shard_map/ppermute | solution.py:98
  18.8 27.3 %all-to-all-start = ((bf16[4,512,192]{1,2,0:T(8,128)(2,1)}), bf16[4,512,192]{1,2,0:T(8,128)(2,1)S(1)}, u32[]{:S(2)}, u32[]{:S(2)}) async-start(bf16[4,512,192]{1,2,0:T(8,128)(2,1)} %broadcast_in_dim.29), calls=%async_computation | async-start | bytes 1572864 | tf_op jit(solution)/shard_map/all_to_all | solution.py:37
  25.8 250.1 %all-gather.3.cloned.1.call-start = ((), (), s32[]{:S(2)}) async-start(), calls=%async_computation.5 | async-start | bytes 4456448 | tf_op jit(solution)/shard_map/all_gather | solution.py:116
  25.8 3.7 %copy-start.23 = (s32[1024,1]{0,1:T(1,128)S(1)}, s32[1024,1]{0,1:T(1,128)}, u32[]{:S(2)}) copy-start(s32[1024,1]{0,1:T(1,128)} %param.16) | copy-start | bytes 12292
  46.2 17.0 %collective-permute-start.1 = (bf16[2048,192]{0,1:T(8,128)(2,1)S(1)}, bf16[2048,192]{0,1:T(8,128)(2,1)}, u32[]{:S(2)}, u32[]{:S(2)}) collective-permute-start(bf16[2048,192]{0,1:T(8,128)(2,1)S(1)} %bitcast.156), channel_id=1, source_target_pairs={{0,128},{128,256},{256,384},{384,0},{1,129},{129,257},{257,385},{3... | collective-permute-start | bytes 2359304 | tf_op jit(solution)/shard_map/ppermute | solution.py:43
  48.1 15.0 %collective-permute-start.2 = (bf16[2048,192]{0,1:T(8,128)(2,1)S(1)}, bf16[2048,192]{0,1:T(8,128)(2,1)}, u32[]{:S(2)}, u32[]{:S(2)}) collective-permute-start(bf16[2048,192]{0,1:T(8,128)(2,1)S(1)} %bitcast.157), channel_id=1, source_target_pairs={{0,384},{128,0},{256,128},{384,256},{1,385},{129,1},{257,129},{385... | collective-permute-start | bytes 2359304 | tf_op jit(solution)/shard_map/ppermute | solution.py:43
  53.2 4.4 %copy-start.1 = (bf16[256,8192]{1,0:T(8,128)(2,1)S(1)}, bf16[256,8192]{1,0:T(8,128)(2,1)}, u32[]{:S(2)}) copy-start(bf16[256,8192]{1,0:T(8,128)(2,1)} %fusion.2) | copy-start | bytes 12582916
  57.7 2.5 copy-start.22
  63.1 12.4 %copy-start.3 = (bf16[32,8,2048]{2,1,0:T(8,128)(2,1)S(1)}, bf16[32,8,2048]{2,1,0:T(8,128)(2,1)}, u32[]{:S(2)}) copy-start(bf16[32,8,2048]{2,1,0:T(8,128)(2,1)} %get-tuple-element.31) | copy-start | bytes 3145732
  64.2 39.5 %collective-permute-start.5 = (bf16[1024,192]{0,1:T(8,128)(2,1)S(1)}, bf16[1024,192]{0,1:T(8,128)(2,1)}, u32[]{:S(2)}, u32[]{:S(2)}) collective-permute-start(bf16[1024,192]{0,1:T(8,128)(2,1)S(1)} %slice.67), channel_id=1, source_target_pairs={{0,128},{128,256},{256,384},{384,0},{1,129},{129,257},{257,385},{3... | collective-permute-start | bytes 1179656 | tf_op jit(solution)/shard_map/ppermute | solution.py:52
  69.1 34.7 %collective-permute-start.6 = (bf16[1024,192]{0,1:T(8,128)(2,1)}, bf16[1024,192]{0,1:T(8,128)(2,1)}, u32[]{:S(2)}, u32[]{:S(2)}) collective-permute-start(bf16[1024,192]{0,1:T(8,128)(2,1)} %slice.68), channel_id=1, source_target_pairs={{0,384},{128,0},{256,128},{384,256},{1,385},{129,1},{257,129},{385... | collective-permute-start | bytes 1179656 | tf_op jit(solution)/shard_map/ppermute | solution.py:52
  75.5 28.3 %copy-start.2 = (bf16[32,8,2048]{2,1,0:T(8,128)(2,1)S(1)}, bf16[32,8,2048]{2,1,0:T(8,128)(2,1)}, u32[]{:S(2)}) copy-start(bf16[32,8,2048]{2,1,0:T(8,128)(2,1)} %get-tuple-element.33) | copy-start | bytes 3145732
  79.8 10.1 %collective-permute-start.7 = (bf16[256,128]{1,0:T(8,128)(2,1)}, bf16[256,128]{1,0:T(8,128)(2,1)}, u32[]{:S(2)}, u32[]{:S(2)}) collective-permute-start(bf16[256,128]{1,0:T(8,128)(2,1)} %slice.69), channel_id=1, source_target_pairs={{0,128},{128,256},{256,384},{384,0},{1,129},{129,257},{257,385},{3... | collective-permute-start | bytes 196616 | tf_op jit(solution)/shard_map/ppermute | solution.py:52
  84.7 7.3 %collective-permute-start.8 = (bf16[256,128]{1,0:T(8,128)(2,1)}, bf16[256,128]{1,0:T(8,128)(2,1)}, u32[]{:S(2)}, u32[]{:S(2)}) collective-permute-start(bf16[256,128]{1,0:T(8,128)(2,1)} %slice.70), channel_id=1, source_target_pairs={{0,384},{128,0},{256,128},{384,256},{1,385},{129,1},{257,129},{385... | collective-permute-start | bytes 196616 | tf_op jit(solution)/shard_map/ppermute | solution.py:52
  95.1 29.5 %collective-permute-start.9 = (bf16[2048,128]{1,0:T(8,128)(2,1)}, bf16[2048,128]{1,0:T(8,128)(2,1)S(1)}, u32[]{:S(2)}, u32[]{:S(2)}) collective-permute-start(bf16[2048,128]{1,0:T(8,128)(2,1)} %constant_dynamic-update-slice_fusion), channel_id=1, source_target_pairs={{0,96},{32,0},{64,32},{96,64},{1,97},{33,1},{65,33},{97,65},{2,98}... | collective-permute-start | bytes 1572872 | tf_op jit(solution)/shard_map/ppermute | solution.py:43
  99.3 23.3 %collective-permute-start.10 = (bf16[2048,128]{1,0:T(8,128)(2,1)}, bf16[2048,128]{1,0:T(8,128)(2,1)S(1)}, u32[]{:S(2)}, u32[]{:S(2)}) collective-permute-start(bf16[2048,128]{1,0:T(8,128)(2,1)} %constant_dynamic-update-slice_fusion), channel_id=1, source_target_pairs={{0,32},{32,64},{64,96},{96,0},{1,33},{33,65},{65,97},{97,1},{2,34}... | collective-permute-start | bytes 1572872 | tf_op jit(solution)/shard_map/ppermute | solution.py:43
  103.8 2.0 copy-start.20
  105.9 23.6 %copy-start.16 = (bf16[256,512]{1,0:T(8,128)(2,1)S(1)}, bf16[256,512]{1,0:T(8,128)(2,1)}, u32[]{:S(2)}) copy-start(bf16[256,512]{1,0:T(8,128)(2,1)} %get-tuple-element.43) | copy-start | bytes 786436
  105.9 23.6 %copy-start.17 = (bf16[256,512]{1,0:T(8,128)(2,1)S(1)}, bf16[256,512]{1,0:T(8,128)(2,1)}, u32[]{:S(2)}) copy-start(bf16[256,512]{1,0:T(8,128)(2,1)} %get-tuple-element.44) | copy-start | bytes 786436
  105.9 23.6 %copy-start.18 = (bf16[256,512]{1,0:T(8,128)(2,1)S(1)}, bf16[256,512]{1,0:T(8,128)(2,1)}, u32[]{:S(2)}) copy-start(bf16[256,512]{1,0:T(8,128)(2,1)} %get-tuple-element.45) | copy-start | bytes 786436
  105.9 23.6 %copy-start.19 = (bf16[256,512]{1,0:T(8,128)(2,1)S(1)}, bf16[256,512]{1,0:T(8,128)(2,1)}, u32[]{:S(2)}) copy-start(bf16[256,512]{1,0:T(8,128)(2,1)} %get-tuple-element.46) | copy-start | bytes 786436
  122.6 16.5 %collective-permute-start.11 = (bf16[1024,128]{1,0:T(8,128)(2,1)S(1)}, bf16[1024,128]{1,0:T(8,128)(2,1)S(1)}, u32[]{:S(2)}, u32[]{:S(2)}) collective-permute-start(bf16[1024,128]{1,0:T(8,128)(2,1)S(1)} %slice.101), channel_id=1, source_target_pairs={{0,32},{32,64},{64,96},{96,0},{1,33},{33,65},{65,97},{97,1},{2,34}... | collective-permute-start | bytes 786440 | tf_op jit(solution)/shard_map/ppermute | solution.py:52
  124.6 14.5 %collective-permute-start.12 = (bf16[1024,128]{1,0:T(8,128)(2,1)S(1)}, bf16[1024,128]{1,0:T(8,128)(2,1)S(1)}, u32[]{:S(2)}, u32[]{:S(2)}) collective-permute-start(bf16[1024,128]{1,0:T(8,128)(2,1)S(1)} %slice.102), channel_id=1, source_target_pairs={{0,96},{32,0},{64,32},{96,64},{1,97},{33,1},{65,33},{97,65},{2,98}... | collective-permute-start | bytes 786440 | tf_op jit(solution)/shard_map/ppermute | solution.py:52
  129.5 1.0 copy-start.12
  129.5 1.0 copy-start.13
  129.5 1.1 copy-start.14
  129.5 1.2 copy-start.15
  130.6 8.5 %copy-start.8 = (bf16[256,512]{1,0:T(8,128)(2,1)S(1)}, bf16[256,512]{1,0:T(8,128)(2,1)}, u32[]{:S(2)}) copy-start(bf16[256,512]{1,0:T(8,128)(2,1)} %get-tuple-element.39) | copy-start | bytes 786436
  130.7 8.5 %copy-start.9 = (bf16[256,512]{1,0:T(8,128)(2,1)S(1)}, bf16[256,512]{1,0:T(8,128)(2,1)}, u32[]{:S(2)}) copy-start(bf16[256,512]{1,0:T(8,128)(2,1)} %get-tuple-element.40) | copy-start | bytes 786436
  130.7 8.5 %copy-start.10 = (bf16[256,512]{1,0:T(8,128)(2,1)S(1)}, bf16[256,512]{1,0:T(8,128)(2,1)}, u32[]{:S(2)}) copy-start(bf16[256,512]{1,0:T(8,128)(2,1)} %get-tuple-element.41) | copy-start | bytes 786436
  130.7 8.5 %copy-start.11 = (bf16[256,512]{1,0:T(8,128)(2,1)S(1)}, bf16[256,512]{1,0:T(8,128)(2,1)}, u32[]{:S(2)}) copy-start(bf16[256,512]{1,0:T(8,128)(2,1)} %get-tuple-element.42) | copy-start | bytes 786436
  139.1 1.0 copy-start.4
  139.2 1.0 copy-start.5
  139.2 1.1 copy-start.6
  139.2 1.2 copy-start.7
  140.3 42.9 %copy-start.24 = (s32[64,1]{0,1:T(1,128)S(1)}, s32[64,1]{0,1:T(1,128)}, u32[]{:S(2)}) copy-start(s32[64,1]{0,1:T(1,128)} %reshape.253) | copy-start | bytes 772
  142.6 54.7 %all-to-all-start.1 = ((bf16[8,32,320]{2,0,1:T(8,128)(2,1)}), bf16[8,32,320]{2,0,1:T(8,128)(2,1)S(1)}, u32[]{:S(2)}, u32[]{:S(2)}) async-start(bf16[8,32,320]{2,0,1:T(8,128)(2,1)} %pad_maximum_fusion), calls=%async_computation.1 | async-start | bytes 393216 | tf_op jit(solution)/shard_map/all_to_all | solution.py:32
  197.4 4.1 %copy-start.25 = (s32[256]{0:T(256)S(1)}, s32[256]{0:T(256)}, u32[]{:S(2)}) copy-start(s32[256]{0:T(256)} %param.15) | copy-start | bytes 3076
  197.4 54.0 %all-to-all-start.2 = ((bf16[32,2,2,8,1024]{4,3,2,1,0:T(8,128)(2,1)}), bf16[32,2,2,8,1024]{4,3,2,1,0:T(8,128)(2,1)S(1)}, u32[]{:S(2)}, u32[]{:S(2)}) async-start(bf16[32,2,2,8,1024]{4,3,2,1,0:T(8,128)(2,1)} %bitcast.30), calls=%async_computation.2 | async-start | bytes 4194304 | tf_op jit(solution)/shard_map/all_to_all | solution.py:161
Sparse Core Ops, SparseCore 0:
  90.0 103.1 all-gather.2
where the time goes:
time: 344 us; the launch traced here: 343 us
  starting transfers between devices  97.2 us (28%)
  waiting for transfers between devices  94.1 us (27%)
  blocking collectives  73.1 us (21%)
  local copies, waits for them, and re-layouts  36.3 us (11%)
  matrix products  14.7 us (4%)
  between operations  14.3 us (4%)
  other arithmetic  13.2 us (4%)
    all_to_all x1, blocking collectives, shards(): spread = lax.all_to_all(partial.transpose(1, 0, 2), PAIR, 0, 0, tiled=True)  53.2 us
    all_to_all x1, waiting for transfers between devices, shards(): lax.all_to_all(outgoing, BEAM, split_axis=0, concat_axis=0, tiled=True)  48.5 us
    all_to_all x1, starting transfers between devices, regroup(): return lax.all_to_all(blocks, BEAM, split_axis=1, concat_axis=1, tiled=True)  40.6 us
    ppermute x6, starting transfers between devices, ring_near(): return (lax.ppermute(piece, axis, ahead), lax.ppermute(piece, axis, behind))  22.8 us
    all_to_all x1, blocking collectives, shards(): lax.all_to_all(doubled.reshape(own_beams, columns, pair_feats.shape[3]),...  19.9 us
    ppermute x6, waiting for transfers between devices, ring_near(): return (lax.ppermute(piece, axis, ahead), lax.ppermute(piece, axis, behind))  14.6 us
    ppermute x3, starting transfers between devices, ring_far(): lax.ppermute(from_right[cut:], axis, behind)  14 us
    all_to_all x1, waiting for transfers between devices, regroup(): return lax.all_to_all(blocks, BEAM, split_axis=1, concat_axis=1, tiled=True)  12 us
  transfers between devices with their start and end apart: 17, of which 6 were waited for; matrix products, arithmetic and copies ran while one was open for 16% of the time, Pallas kernels for 0%

commit v1 on v0

--- a/solution.py
+++ b/solution.py
@@ -180,8 +180,20 @@
     pairs = columns // cores
     pair_feats = attn.reshape(own_beams, pairs, 1, cores * attn.shape[1] // columns)
     doubled = jnp.broadcast_to(pair_feats, (own_beams, pairs, cores, pair_feats.shape[3]))
-    head_rows = lax.all_to_all(
-        doubled.reshape(own_beams, columns, pair_feats.shape[3]), BEAM, 1, 1, tiled=True
+    head_rows = jnp.concatenate(
+        lax.all_to_all(
+            jnp.stack(
+                jnp.split(
+                    doubled.reshape(own_beams, columns, pair_feats.shape[3]),
+                    lax.axis_size(BEAM),
+                    axis=1,
+                )
+            ),
+            BEAM,
+            0,
+            0,
+        ),
+        axis=1,
     )
     block = attn.shape[1] // columns
     partial = None

time: 344 us -> 331 us (0.962)
  blocking collectives: 73.1 us -> 89.9 us
  starting transfers between devices: 97.2 us -> 80.6 us
  local copies, waits for them, and re-layouts: 36.3 us -> 30.4 us
  waiting for transfers between devices: 94.1 us -> 88.3 us
    all_to_all x1, starting transfers between devices: 40.6 us -> 22.4 us  [regroup(): return lax.all_to_all(blocks, BEAM, split_axis=1, concat_axis=1, tiled=True)]
    all_to_all x1, blocking collectives: 19.9 us -> 29.8 us  [shards(): lax.all_to_all(jnp.stack(jnp.split(doubled.reshape(own_beams, columns, pa...]
    all_to_all x1, blocking collectives: 53.2 us -> 60 us  [shards(): spread = lax.all_to_all(partial.transpose(1, 0, 2), PAIR, 0, 0, tiled=True)]
    ppermute x3, waiting for transfers between devices: 8.01 us -> 2.75 us  [ring_far(): lax.ppermute(from_left[:cut], axis, ahead)]
    all_to_all x1, waiting for transfers between devices: 12 us -> 7.87 us  [regroup(): return lax.all_to_all(blocks, BEAM, split_axis=1, concat_axis=1, tiled=True)]
    all_gather x1, waiting for transfers between devices: 0.02 us -> 3.74 us  [shards(): w_pair = lax.all_gather(w_local[:, None], OWNER, axis=1, tiled=True)]
    unnamed x60 -> x91, local copies, waits for them, and re-layouts: 9.86 us -> 6.5 us
  transfers between devices with their start and end apart: 17 -> 17, of which waited for: 6 -> 8; matrix products, arithmetic and copies ran while one was open for 16% -> 13% of each run, Pallas kernels for 0% -> 0%
where the time goes in v1:
time: 331 us; the launch traced here: 329 us
  blocking collectives  89.9 us (27%)
  waiting for transfers between devices  88.3 us (27%)
  starting transfers between devices  80.6 us (24%)
  local copies, waits for them, and re-layouts  30.4 us (9%)
  between operations  14.5 us (4%)
  other arithmetic  13.3 us (4%)
  matrix products  11.8 us (4%)
    all_to_all x1, blocking collectives, shards(): spread = lax.all_to_all(partial.transpose(1, 0, 2), PAIR, 0, 0, tiled=True)  60 us
    all_to_all x1, waiting for transfers between devices, shards(): lax.all_to_all(outgoing, BEAM, split_axis=0, concat_axis=0, tiled=True)  48.4 us
    all_to_all x1, blocking collectives, shards(): lax.all_to_all(jnp.stack(jnp.split(doubled.reshape(own_beams, columns, pa...  29.8 us
    ppermute x6, starting transfers between devices, ring_near(): return (lax.ppermute(piece, axis, ahead), lax.ppermute(piece, axis, behind))  22.8 us
    all_to_all x1, starting transfers between devices, regroup(): return lax.all_to_all(blocks, BEAM, split_axis=1, concat_axis=1, tiled=True)  22.4 us
    ppermute x3, starting transfers between devices, ring_far(): lax.ppermute(from_right[cut:], axis, behind)  13.7 us
    ppermute x6, waiting for transfers between devices, ring_near(): return (lax.ppermute(piece, axis, ahead), lax.ppermute(piece, axis, behind))  12 us
    all_to_all x1, waiting for transfers between devices, gather_rows(): lax.all_to_all(copies, axis, 0, 0, tiled=True)  10.3 us
  transfers between devices with their start and end apart: 17, of which 8 were waited for; matrix products, arithmetic and copies ran while one was open for 13% of the time, Pallas kernels for 0%

profile of v1, /device:TPU:56, one launch (start us, length us, event | category | flops | bytes accessed | tf_op | source)
XLA Modules:
  0.0 328.8 jit_solution(15406604925702332585)
XLA Ops:
  6.5 1.0 slice.65
  7.7 3.4 %collective-permute-start.3 = (bf16[512,128]{1,0:T(8,128)(2,1)S(1)}, bf16[512,128]{1,0:T(8,128)(2,1)}, u32[]{:S(2)}, u32[]{:S(2)}) collective-permute-start(bf16[512,128]{1,0:T(8,128)(2,1)S(1)} %copy.1928), channel_id=1, source_target_pairs={{0,128},{128,256},{256,384},{384,0},{1,129},{129,257},{257,385},{3... | collective-permute-start | bytes 393224 | tf_op jit(solution)/shard_map/ppermute | solution.py:43
  11.1 3.7 %collective-permute-start.4 = (bf16[512,128]{1,0:T(8,128)(2,1)S(1)}, bf16[512,128]{1,0:T(8,128)(2,1)}, u32[]{:S(2)}, u32[]{:S(2)}) collective-permute-start(bf16[512,128]{1,0:T(8,128)(2,1)S(1)} %copy.1928), channel_id=1, source_target_pairs={{0,384},{128,0},{256,128},{384,256},{1,385},{129,1},{257,129},{385... | collective-permute-start | bytes 393224 | tf_op jit(solution)/shard_map/ppermute | solution.py:43
  14.8 1.1 copy.1879
  15.9 1.9 collective-permute-start
  17.9 1.0 broadcast_in_dim.29
  18.8 7.0 %all-to-all-start = ((bf16[4,512,192]{1,2,0:T(8,128)(2,1)}), bf16[4,512,192]{1,2,0:T(8,128)(2,1)S(1)}, u32[]{:S(2)}, u32[]{:S(2)}) async-start(bf16[4,512,192]{1,2,0:T(8,128)(2,1)} %broadcast_in_dim.29), calls=%async_computation | async-start | bytes 1572864 | tf_op jit(solution)/shard_map/all_to_all | solution.py:37
  25.8 3.1 fusion
  30.4 5.3 %fusion.2 = bf16[256,8192]{1,0:T(8,128)(2,1)} fusion(bf16[256,8192]{1,0:T(8,128)(2,1)} %param.10, f32[8192]{0:T(1024)S(1)} %convert_element_type.98, f32[256]{0:T(256)S(1)} %add_rsqrt_fusion), kind=kLoop, calls=%fused_computation.6 | loop fusion | flops 8388608 | bytes 8422400 | tf_op jit(solution)/shard_map/convert_element_type | solution.py:104
  35.8 10.3 %all-to-all-done = bf16[4,512,192]{1,2,0:T(8,128)(2,1)S(1)} async-done(((bf16[4,512,192]{1,2,0:T(8,128)(2,1)}), bf16[4,512,192]{1,2,0:T(8,128)(2,1)S(1)}, u32[]{:S(2)}, u32[]{:S(2)}) %all-to-all-start) | async-done | bytes 786464 | tf_op jit(solution)/shard_map/all_to_all | solution.py:37
  46.2 1.9 collective-permute-start.1
  48.1 5.1 %collective-permute-start.2 = (bf16[2048,192]{0,1:T(8,128)(2,1)S(1)}, bf16[2048,192]{0,1:T(8,128)(2,1)}, u32[]{:S(2)}, u32[]{:S(2)}) collective-permute-start(bf16[2048,192]{0,1:T(8,128)(2,1)S(1)} %bitcast.323), channel_id=1, source_target_pairs={{0,384},{128,0},{256,128},{384,256},{1,385},{129,1},{257,129},{385... | collective-permute-start | bytes 2359304 | tf_op jit(solution)/shard_map/ppermute | solution.py:43
  53.3 4.5 %constant_dynamic-slice_fusion.16 = (bf16[256,512]{1,0:T(8,128)(2,1)}, bf16[256,512]{1,0:T(8,128)(2,1)}, bf16[256,512]{1,0:T(8,128)(2,1)}, bf16[256,512]{1,0:T(8...) fusion(bf16[256,8192]{1,0:T(8,128)(2,1)} %fusion.2, ...), kind=kLoop, calls=%fused_computation.210 | loop fusion | bytes 8388672 | tf_op jit(solution)/shard_map/dynamic_slice | solution.py:135
  57.8 1.7 dynamic-slice_bitcast_fusion.2
  63.2 1.1 slice.67
  64.3 3.0 collective-permute-start.5
  67.3 1.0 slice.68
  68.4 4.0 %collective-permute-start.6 = (bf16[1024,192]{0,1:T(8,128)(2,1)S(1)}, bf16[1024,192]{0,1:T(8,128)(2,1)S(1)}, u32[]{:S(2)}, u32[]{:S(2)}) collective-permute-start(bf16[1024,192]{0,1:T(8,128)(2,1)S(1)} %slice.68), channel_id=1, source_target_pairs={{0,384},{128,0},{256,128},{384,256},{1,385},{129,1},{257,129},{385... | collective-permute-start | bytes 1179656 | tf_op jit(solution)/shard_map/ppermute | solution.py:52
  72.4 2.4 fusion.42
  74.8 2.1 fusion.46
  77.8 1.9 collective-permute-start.7
  79.7 0.9 constant_dynamic-update-slice_fusion.3
  80.6 0.8 slice.70
  81.5 5.1 %collective-permute-start.8 = (bf16[256,128]{1,0:T(8,128)(2,1)S(1)}, bf16[256,128]{1,0:T(8,128)(2,1)S(1)}, u32[]{:S(2)}, u32[]{:S(2)}) collective-permute-start(bf16[256,128]{1,0:T(8,128)(2,1)S(1)} %slice.70), channel_id=1, source_target_pairs={{0,384},{128,0},{256,128},{384,256},{1,385},{129,1},{257,129},{385... | collective-permute-start | bytes 196616 | tf_op jit(solution)/shard_map/ppermute | solution.py:52
  86.6 1.9 collective-permute-done.8
  88.5 0.9 constant_dynamic-update-slice_fusion
  89.4 4.2 %collective-permute-start.9 = (bf16[2048,128]{1,0:T(8,128)(2,1)S(1)}, bf16[2048,128]{1,0:T(8,128)(2,1)S(1)}, u32[]{:S(2)}, u32[]{:S(2)}) collective-permute-start(bf16[2048,128]{1,0:T(8,128)(2,1)S(1)} %constant_dynamic-update-slice_fusion), channel_id=1, source_target_pairs={{0,96},{32,0},{64,32},{96,64},{1,97},{33,1},{65,33},{97,65},{2,98}... | collective-permute-start | bytes 1572872 | tf_op jit(solution)/shard_map/ppermute | solution.py:43
  93.7 4.5 %collective-permute-start.10 = (bf16[2048,128]{1,0:T(8,128)(2,1)S(1)}, bf16[2048,128]{1,0:T(8,128)(2,1)S(1)}, u32[]{:S(2)}, u32[]{:S(2)}) collective-permute-start(bf16[2048,128]{1,0:T(8,128)(2,1)S(1)} %constant_dynamic-update-slice_fusion), channel_id=1, source_target_pairs={{0,32},{32,64},{64,96},{96,0},{1,33},{33,65},{65,97},{97,1},{2,34}... | collective-permute-start | bytes 1572872 | tf_op jit(solution)/shard_map/ppermute | solution.py:43
  98.2 0.9 fusion.44
  99.1 2.1 fusion.8
  101.2 12.0 %collective-permute-done.10 = bf16[2048,128]{1,0:T(8,128)(2,1)S(1)} collective-permute-done((bf16[2048,128]{1,0:T(8,128)(2,1)S(1)}, bf16[2048,128]{1,0:T(8,128)(2,1)S(1)}, u32[]{:S(2)}, u32[]{:S(2)}) %collective-permute-start.10) | collective-permute-done | bytes 524320 | tf_op jit(solution)/shard_map/ppermute | solution.py:43
  113.2 3.6 %collective-permute-start.11 = (bf16[1024,128]{1,0:T(8,128)(2,1)S(1)}, bf16[1024,128]{1,0:T(8,128)(2,1)S(1)}, u32[]{:S(2)}, u32[]{:S(2)}) collective-permute-start(bf16[1024,128]{1,0:T(8,128)(2,1)S(1)} %slice.101), channel_id=1, source_target_pairs={{0,32},{32,64},{64,96},{96,0},{1,33},{33,65},{65,97},{97,1},{2,34}... | collective-permute-start | bytes 786440 | tf_op jit(solution)/shard_map/ppermute | solution.py:52
  116.8 4.5 %collective-permute-start.12 = (bf16[1024,128]{1,0:T(8,128)(2,1)S(1)}, bf16[1024,128]{1,0:T(8,128)(2,1)S(1)}, u32[]{:S(2)}, u32[]{:S(2)}) collective-permute-start(bf16[1024,128]{1,0:T(8,128)(2,1)S(1)} %slice.102), channel_id=1, source_target_pairs={{0,96},{32,0},{64,32},{96,64},{1,97},{33,1},{65,33},{97,65},{2,98}... | collective-permute-start | bytes 786440 | tf_op jit(solution)/shard_map/ppermute | solution.py:52
  123.1 2.7 collective-permute-done.11
  125.8 1.4 collective-permute-done.12
  129.7 22.4 %all-to-all-start.1 = ((bf16[8,32,320]{2,0,1:T(8,128)(2,1)}), bf16[8,32,320]{2,0,1:T(8,128)(2,1)S(1)}, u32[]{:S(2)}, u32[]{:S(2)}) async-start(bf16[8,32,320]{2,0,1:T(8,128)(2,1)} %pad_maximum_fusion), calls=%async_computation.1 | async-start | bytes 393216 | tf_op jit(solution)/shard_map/all_to_all | solution.py:32
  152.1 2.1 gather_fusion
  154.2 7.9 %all-to-all-done.1 = bf16[8,32,320]{2,0,1:T(8,128)(2,1)S(1)} async-done(((bf16[8,32,320]{2,0,1:T(8,128)(2,1)}), bf16[8,32,320]{2,0,1:T(8,128)(2,1)S(1)}, u32[]{:S(2)}, u32[]{:S(2)}) %all-to-all-start.1) | async-done | bytes 163872 | tf_op jit(solution)/shard_map/all_to_all | solution.py:32
  162.1 4.3 %all-to-all-start.2 = ((bf16[32,2,2,8,1024]{4,3,2,1,0:T(8,128)(2,1)}), bf16[32,2,2,8,1024]{4,3,2,1,0:T(8,128)(2,1)S(1)}, u32[]{:S(2)}, u32[]{:S(2)}) async-start(bf16[32,2,2,8,1024]{4,3,2,1,0:T(8,128)(2,1)} %bitcast.30), calls=%async_computation.2 | async-start | bytes 4194304 | tf_op jit(solution)/shard_map/all_to_all | solution.py:161
  168.0 48.4 %all-to-all-done.2 = bf16[32,2,2,8,1024]{4,3,2,1,0:T(8,128)(2,1)S(1)} async-done(((bf16[32,2,2,8,1024]{4,3,2,1,0:T(8,128)(2,1)}), bf16[32,2,2,8,1024]{4,3,2,1,0:T(8,128)(2,1)S(1)}, u32[]{:S(2)}, u32[]{:S(2)}) %all-to-all-start.2) | async-done | bytes 2097184 | tf_op jit(solution)/shard_map/all_to_all | solution.py:161
  216.4 1.6 gather_fusion.1
  218.0 1.6 copy.1930
  221.4 29.8 %all_to_all.25 = bf16[32,8,1,512]{3,1,2,0:T(8,128)(2,1)S(1)} all-to-all(bf16[32,8,1,512]{3,1,2,0:T(8,128)(2,1)S(1)} %constant_dynamic-update-slice_fusion.5), channel_id=1, replica_groups=mesh['x'=4,'yh'=4,'yl'=2,'z'=8,'c'=2] {'yl','z','c'}, dimensions={0} | all-to-all | bytes 524288 | tf_op jit(solution)/shard_map/all_to_all | solution.py:184
  251.3 3.7 %all-gather.3.cloned.1.call-done = bf16[512,4096]{0,1:T(8,128)(2,1)} async-done(((bf16[512,256]{0,1:T(8,128)(2,1)}), bf16[512,4096]{0,1:T(8,128)(2,1)}) %all-gather.3.cloned.1.call-update) | async-done | bytes 4194320 | tf_op jit(solution)/shard_map/all_gather | solution.py:116
  255.1 2.5 fusion.89
  259.1 1.2 copy.1909
  261.0 60.0 %all_to_all.26 = bf16[16,256,256]{2,1,0:T(8,128)(2,1)S(1)} all-to-all(bf16[16,256,256]{2,1,0:T(8,128)(2,1)S(1)} %copy.1910), channel_id=1, replica_groups=mesh['x'=4,'yh'=4,'yl'=2,'z'=8,'c'=2] {'yl','z'}, dimensions={0} | all-to-all | bytes 4194304 | tf_op jit(solution)/shard_map/all_to_all | solution.py:213
  321.0 1.0 reduce_sum.55
  (161 shorter events, 15.7 us)
Async XLA Ops:
  6.5 145.6 %copy-start = (bf16[32,2,8,1024]{3,2,1,0:T(8,128)(2,1)S(1)}, bf16[32,2,8,1024]{3,2,1,0:T(8,128)(2,1)}, u32[]{:S(2)}) copy-start(bf16[32,2,8,1024]{3,2,1,0:T(8,128)(2,1)} %param.14) | copy-start | bytes 3145732
  6.5 11.3 %slice-start = ((bf16[512,320]{0,1:T(8,128)(2,1)}), bf16[512,192]{0,1:T(8,128)(2,1)S(1)}, s32[]{:S(2)}) async-start(bf16[512,320]{0,1:T(8,128)(2,1)} %param.12), calls=%async_computation.6 | async-start | bytes 393216 | tf_op jit(solution)/shard_map/slice | solution.py:112
  7.7 55.5 %collective-permute-start.3 = (bf16[512,128]{1,0:T(8,128)(2,1)S(1)}, bf16[512,128]{1,0:T(8,128)(2,1)}, u32[]{:S(2)}, u32[]{:S(2)}) collective-permute-start(bf16[512,128]{1,0:T(8,128)(2,1)S(1)} %copy.1928), channel_id=1, source_target_pairs={{0,128},{128,256},{256,384},{384,0},{1,129},{129,257},{257,385},{3... | collective-permute-start | bytes 393224 | tf_op jit(solution)/shard_map/ppermute | solution.py:43
  11.1 52.1 %collective-permute-start.4 = (bf16[512,128]{1,0:T(8,128)(2,1)S(1)}, bf16[512,128]{1,0:T(8,128)(2,1)}, u32[]{:S(2)}, u32[]{:S(2)}) collective-permute-start(bf16[512,128]{1,0:T(8,128)(2,1)S(1)} %copy.1928), channel_id=1, source_target_pairs={{0,384},{128,0},{256,128},{384,256},{1,385},{129,1},{257,129},{385... | collective-permute-start | bytes 393224 | tf_op jit(solution)/shard_map/ppermute | solution.py:43
  14.8 11.0 %copy-start.21 = (bf16[8192]{0:T(1024)(128)(2,1)S(1)}, bf16[8192]{0:T(1024)(128)(2,1)}, u32[]{:S(2)}) copy-start(bf16[8192]{0:T(1024)(128)(2,1)} %param.11) | copy-start | bytes 49156
  15.9 45.2 %collective-permute-start = (bf16[256,256]{0,1:T(8,128)(2,1)S(1)}, bf16[256,256]{0,1:T(8,128)(2,1)S(1)}, u32[]{:S(2)}, u32[]{:S(2)}) collective-permute-start(bf16[256,256]{0,1:T(8,128)(2,1)S(1)} %get-tuple-element.55), channel_id=1, source_target_pairs={{0,1},{1,0},{2,3},{3,2},{4,5},{5,4},{6,7},{7,6},{8,9},{9,8},{10,11... | collective-permute-start | bytes 393224 | tf_op jit(solution)/shard_map/ppermute | solution.py:98
  18.8 27.3 %all-to-all-start = ((bf16[4,512,192]{1,2,0:T(8,128)(2,1)}), bf16[4,512,192]{1,2,0:T(8,128)(2,1)S(1)}, u32[]{:S(2)}, u32[]{:S(2)}) async-start(bf16[4,512,192]{1,2,0:T(8,128)(2,1)} %broadcast_in_dim.29), calls=%async_computation | async-start | bytes 1572864 | tf_op jit(solution)/shard_map/all_to_all | solution.py:37
  25.8 3.7 %copy-start.23 = (s32[1024,1]{0,1:T(1,128)S(1)}, s32[1024,1]{0,1:T(1,128)}, u32[]{:S(2)}) copy-start(s32[1024,1]{0,1:T(1,128)} %param.16) | copy-start | bytes 12292
  46.2 17.0 %collective-permute-start.1 = (bf16[2048,192]{0,1:T(8,128)(2,1)S(1)}, bf16[2048,192]{0,1:T(8,128)(2,1)}, u32[]{:S(2)}, u32[]{:S(2)}) collective-permute-start(bf16[2048,192]{0,1:T(8,128)(2,1)S(1)} %bitcast.322), channel_id=1, source_target_pairs={{0,128},{128,256},{256,384},{384,0},{1,129},{129,257},{257,385},{3... | collective-permute-start | bytes 2359304 | tf_op jit(solution)/shard_map/ppermute | solution.py:43
  48.1 15.1 %collective-permute-start.2 = (bf16[2048,192]{0,1:T(8,128)(2,1)S(1)}, bf16[2048,192]{0,1:T(8,128)(2,1)}, u32[]{:S(2)}, u32[]{:S(2)}) collective-permute-start(bf16[2048,192]{0,1:T(8,128)(2,1)S(1)} %bitcast.323), channel_id=1, source_target_pairs={{0,384},{128,0},{256,128},{384,256},{1,385},{129,1},{257,129},{385... | collective-permute-start | bytes 2359304 | tf_op jit(solution)/shard_map/ppermute | solution.py:43
  53.2 4.6 %copy-start.1 = (bf16[256,8192]{1,0:T(8,128)(2,1)S(1)}, bf16[256,8192]{1,0:T(8,128)(2,1)}, u32[]{:S(2)}) copy-start(bf16[256,8192]{1,0:T(8,128)(2,1)} %fusion.2) | copy-start | bytes 12582916
  57.8 2.4 copy-start.22
  63.2 11.7 %copy-start.3 = (bf16[32,8,2048]{2,1,0:T(8,128)(2,1)S(1)}, bf16[32,8,2048]{2,1,0:T(8,128)(2,1)}, u32[]{:S(2)}) copy-start(bf16[32,8,2048]{2,1,0:T(8,128)(2,1)} %get-tuple-element.31) | copy-start | bytes 3145732
  64.3 33.8 %collective-permute-start.5 = (bf16[1024,192]{0,1:T(8,128)(2,1)S(1)}, bf16[1024,192]{0,1:T(8,128)(2,1)S(1)}, u32[]{:S(2)}, u32[]{:S(2)}) collective-permute-start(bf16[1024,192]{0,1:T(8,128)(2,1)S(1)} %slice.67), channel_id=1, source_target_pairs={{0,128},{128,256},{256,384},{384,0},{1,129},{129,257},{257,385},{3... | collective-permute-start | bytes 1179656 | tf_op jit(solution)/shard_map/ppermute | solution.py:52
  68.4 29.8 %collective-permute-start.6 = (bf16[1024,192]{0,1:T(8,128)(2,1)S(1)}, bf16[1024,192]{0,1:T(8,128)(2,1)S(1)}, u32[]{:S(2)}, u32[]{:S(2)}) collective-permute-start(bf16[1024,192]{0,1:T(8,128)(2,1)S(1)} %slice.68), channel_id=1, source_target_pairs={{0,384},{128,0},{256,128},{384,256},{1,385},{129,1},{257,129},{385... | collective-permute-start | bytes 1179656 | tf_op jit(solution)/shard_map/ppermute | solution.py:52
  72.4 7.3 %copy-start.20 = (bf16[2048,128]{1,0:T(8,128)(2,1)S(1)}, bf16[2048,128]{1,0:T(8,128)(2,1)}, u32[]{:S(2)}) copy-start(bf16[2048,128]{1,0:T(8,128)(2,1)} %constant_dynamic-update-slice_fusion.4) | copy-start | bytes 1572868
  74.8 23.4 %copy-start.2 = (bf16[32,8,2048]{2,1,0:T(8,128)(2,1)S(1)}, bf16[32,8,2048]{2,1,0:T(8,128)(2,1)}, u32[]{:S(2)}) copy-start(bf16[32,8,2048]{2,1,0:T(8,128)(2,1)} %get-tuple-element.33) | copy-start | bytes 3145732
  77.8 8.8 %collective-permute-start.7 = (bf16[256,128]{1,0:T(8,128)(2,1)S(1)}, bf16[256,128]{1,0:T(8,128)(2,1)S(1)}, u32[]{:S(2)}, u32[]{:S(2)}) collective-permute-start(bf16[256,128]{1,0:T(8,128)(2,1)S(1)} %slice.69), channel_id=1, source_target_pairs={{0,128},{128,256},{256,384},{384,0},{1,129},{129,257},{257,385},{3... | collective-permute-start | bytes 196616 | tf_op jit(solution)/shard_map/ppermute | solution.py:52
  81.5 7.0 %collective-permute-start.8 = (bf16[256,128]{1,0:T(8,128)(2,1)S(1)}, bf16[256,128]{1,0:T(8,128)(2,1)S(1)}, u32[]{:S(2)}, u32[]{:S(2)}) collective-permute-start(bf16[256,128]{1,0:T(8,128)(2,1)S(1)} %slice.70), channel_id=1, source_target_pairs={{0,384},{128,0},{256,128},{384,256},{1,385},{129,1},{257,129},{385... | collective-permute-start | bytes 196616 | tf_op jit(solution)/shard_map/ppermute | solution.py:52
  89.4 27.3 %collective-permute-start.9 = (bf16[2048,128]{1,0:T(8,128)(2,1)S(1)}, bf16[2048,128]{1,0:T(8,128)(2,1)S(1)}, u32[]{:S(2)}, u32[]{:S(2)}) collective-permute-start(bf16[2048,128]{1,0:T(8,128)(2,1)S(1)} %constant_dynamic-update-slice_fusion), channel_id=1, source_target_pairs={{0,96},{32,0},{64,32},{96,64},{1,97},{33,1},{65,33},{97,65},{2,98}... | collective-permute-start | bytes 1572872 | tf_op jit(solution)/shard_map/ppermute | solution.py:43
  93.7 19.5 %collective-permute-start.10 = (bf16[2048,128]{1,0:T(8,128)(2,1)S(1)}, bf16[2048,128]{1,0:T(8,128)(2,1)S(1)}, u32[]{:S(2)}, u32[]{:S(2)}) collective-permute-start(bf16[2048,128]{1,0:T(8,128)(2,1)S(1)} %constant_dynamic-update-slice_fusion), channel_id=1, source_target_pairs={{0,32},{32,64},{64,96},{96,0},{1,33},{33,65},{65,97},{97,1},{2,34}... | collective-permute-start | bytes 1572872 | tf_op jit(solution)/shard_map/ppermute | solution.py:43
  99.1 22.3 %copy-start.16 = (bf16[256,512]{1,0:T(8,128)(2,1)S(1)}, bf16[256,512]{1,0:T(8,128)(2,1)}, u32[]{:S(2)}) copy-start(bf16[256,512]{1,0:T(8,128)(2,1)} %get-tuple-element.43) | copy-start | bytes 786436
  99.1 22.3 %copy-start.17 = (bf16[256,512]{1,0:T(8,128)(2,1)S(1)}, bf16[256,512]{1,0:T(8,128)(2,1)}, u32[]{:S(2)}) copy-start(bf16[256,512]{1,0:T(8,128)(2,1)} %get-tuple-element.44) | copy-start | bytes 786436
  99.1 22.3 %copy-start.18 = (bf16[256,512]{1,0:T(8,128)(2,1)S(1)}, bf16[256,512]{1,0:T(8,128)(2,1)}, u32[]{:S(2)}) copy-start(bf16[256,512]{1,0:T(8,128)(2,1)} %get-tuple-element.45) | copy-start | bytes 786436
  99.1 22.3 %copy-start.19 = (bf16[256,512]{1,0:T(8,128)(2,1)S(1)}, bf16[256,512]{1,0:T(8,128)(2,1)}, u32[]{:S(2)}) copy-start(bf16[256,512]{1,0:T(8,128)(2,1)} %get-tuple-element.46) | copy-start | bytes 786436
  113.2 12.6 %collective-permute-start.11 = (bf16[1024,128]{1,0:T(8,128)(2,1)S(1)}, bf16[1024,128]{1,0:T(8,128)(2,1)S(1)}, u32[]{:S(2)}, u32[]{:S(2)}) collective-permute-start(bf16[1024,128]{1,0:T(8,128)(2,1)S(1)} %slice.101), channel_id=1, source_target_pairs={{0,32},{32,64},{64,96},{96,0},{1,33},{33,65},{65,97},{97,1},{2,34}... | collective-permute-start | bytes 786440 | tf_op jit(solution)/shard_map/ppermute | solution.py:52
  116.8 10.4 %collective-permute-start.12 = (bf16[1024,128]{1,0:T(8,128)(2,1)S(1)}, bf16[1024,128]{1,0:T(8,128)(2,1)S(1)}, u32[]{:S(2)}, u32[]{:S(2)}) collective-permute-start(bf16[1024,128]{1,0:T(8,128)(2,1)S(1)} %slice.102), channel_id=1, source_target_pairs={{0,96},{32,0},{64,32},{96,64},{1,97},{33,1},{65,33},{97,65},{2,98}... | collective-permute-start | bytes 786440 | tf_op jit(solution)/shard_map/ppermute | solution.py:52
  121.4 1.0 copy-start.12
  121.4 1.0 copy-start.13
  121.4 1.1 copy-start.14
  121.4 1.2 copy-start.15
  122.6 4.6 %copy-start.8 = (bf16[256,512]{1,0:T(8,128)(2,1)S(1)}, bf16[256,512]{1,0:T(8,128)(2,1)}, u32[]{:S(2)}) copy-start(bf16[256,512]{1,0:T(8,128)(2,1)} %get-tuple-element.39) | copy-start | bytes 786436
  122.6 4.6 %copy-start.9 = (bf16[256,512]{1,0:T(8,128)(2,1)S(1)}, bf16[256,512]{1,0:T(8,128)(2,1)}, u32[]{:S(2)}) copy-start(bf16[256,512]{1,0:T(8,128)(2,1)} %get-tuple-element.40) | copy-start | bytes 786436
  122.6 4.6 %copy-start.10 = (bf16[256,512]{1,0:T(8,128)(2,1)S(1)}, bf16[256,512]{1,0:T(8,128)(2,1)}, u32[]{:S(2)}) copy-start(bf16[256,512]{1,0:T(8,128)(2,1)} %get-tuple-element.41) | copy-start | bytes 786436
  122.6 4.6 %copy-start.11 = (bf16[256,512]{1,0:T(8,128)(2,1)S(1)}, bf16[256,512]{1,0:T(8,128)(2,1)}, u32[]{:S(2)}) copy-start(bf16[256,512]{1,0:T(8,128)(2,1)} %get-tuple-element.42) | copy-start | bytes 786436
  127.2 1.0 copy-start.4
  127.2 1.0 copy-start.5
  127.2 1.1 copy-start.6
  127.2 1.2 copy-start.7
  128.4 23.7 %copy-start.24 = (s32[64,1]{0,1:T(1,128)S(1)}, s32[64,1]{0,1:T(1,128)}, u32[]{:S(2)}) copy-start(s32[64,1]{0,1:T(1,128)} %reshape.259) | copy-start | bytes 772
  129.7 32.4 %all-to-all-start.1 = ((bf16[8,32,320]{2,0,1:T(8,128)(2,1)}), bf16[8,32,320]{2,0,1:T(8,128)(2,1)S(1)}, u32[]{:S(2)}, u32[]{:S(2)}) async-start(bf16[8,32,320]{2,0,1:T(8,128)(2,1)} %pad_maximum_fusion), calls=%async_computation.1 | async-start | bytes 393216 | tf_op jit(solution)/shard_map/all_to_all | solution.py:32
  162.1 4.5 %copy-start.25 = (s32[256]{0:T(256)S(1)}, s32[256]{0:T(256)}, u32[]{:S(2)}) copy-start(s32[256]{0:T(256)} %param.15) | copy-start | bytes 3076
  162.1 54.3 %all-to-all-start.2 = ((bf16[32,2,2,8,1024]{4,3,2,1,0:T(8,128)(2,1)}), bf16[32,2,2,8,1024]{4,3,2,1,0:T(8,128)(2,1)S(1)}, u32[]{:S(2)}, u32[]{:S(2)}) async-start(bf16[32,2,2,8,1024]{4,3,2,1,0:T(8,128)(2,1)} %bitcast.30), calls=%async_computation.2 | async-start | bytes 4194304 | tf_op jit(solution)/shard_map/all_to_all | solution.py:161
  166.3 88.7 %all-gather.3.cloned.1.call-start = ((), (), s32[]{:S(2)}) async-start(), calls=%async_computation.5 | async-start | bytes 4456448 | tf_op jit(solution)/shard_map/all_gather | solution.py:116
Sparse Core Ops, SparseCore 0:
  170.2 84.8 all-gather.2
